TPU v7x, 256 devices: a whole 4x4x8 slice. The times are simulated.
256 devices in a mesh: ctx: 16 (over x_lo, z), fsdp: 4 (over y), head: 4 (over x_hi, core).
Axes of the slice: x: 4 (x_hi: 2, x_lo: 2; x = x_hi * 2 + x_lo), y: 4, z: 8, core: 2. Of those that a mesh axis runs over, the one named last changes fastest.
Arguments:
- queries: bfloat16 [4, 8192, 2048], P('fsdp', 'ctx', 'head'), may hold values from -6 to 6
- keys: bfloat16 [4, 8192, 2048], P('fsdp', 'ctx', 'head'), may hold values from -6 to 6
- values: bfloat16 [4, 8192, 2048], P('fsdp', 'ctx', 'head'), may hold values from -6 to 6
- gate_pre: bfloat16 [4, 8192, 2048], P('fsdp', 'ctx', 'head'), may hold values from -6 to 6
- log_decay: float32 [4, 8192, 16], P('fsdp', 'ctx', 'head'), may hold values from -2 to 0, as said below
- out_grad: bfloat16 [4, 8192, 4096], P('fsdp', 'ctx', 'head'), may hold values from -6 to 6
- out_weight: float32 [4096, 2048], P(('ctx', 'fsdp'), 'head'), may hold values from -0.125 to 0.125
- moment_one: float32 [4096, 2048], P(('ctx', 'fsdp'), 'head'), may hold values from -2 to 2
- moment_two: float32 [4096, 2048], P(('ctx', 'fsdp'), 'head'), may hold values from 0.05 to 1
- group_ids: int32 [128], P(('ctx', 'fsdp')), may hold values from 0 to 2
- step_count: int32 [1], replicated, may hold values from 1 to 40
Outputs:
- query_grad: bfloat16 [4, 8192, 2048], P('fsdp', 'ctx', 'head')
- key_grad: bfloat16 [4, 8192, 2048], P('fsdp', 'ctx', 'head')
- value_grad: bfloat16 [4, 8192, 2048], P('fsdp', 'ctx', 'head')
- new_moment_one: float32 [4096, 2048], P(('ctx', 'fsdp'), 'head')
- new_moment_two: float32 [4096, 2048], P(('ctx', 'fsdp'), 'head')
- weight_step: float32 [4096, 2048], P(('ctx', 'fsdp'), 'head')
Inputs may be any that keep to these rules, and one draw needn't show every extreme that they name: `log_decay`: Log-decays per token and head, never positive. `group_ids`: 0 for a frozen block of rows, 1 for one updated without weight decay, 2 for one updated with it.
All inputs are finite; a program needn't handle non-finite values.
Results may differ from a plain program's by a relative error of at most 0.017.
Values may be sent and summed in bfloat16 or wider, within the bound.
No kernel may reach another device: no remote copies, remote signals or barrier semaphores. Data moves between devices by JAX's collectives and lax.ppermute only.
A program may use at most 128 MiB of HBM per device.

v0:
```python
import jax
import jax.numpy as jnp
from jax import lax
from jax.sharding import PartitionSpec as P

HEAD_DIM = 128
SPAN = 256
ROW_BLOCK = 32
NORM_EPS = 1e-06
BETA_ONE = 0.9
BETA_TWO = 0.95
ADAM_EPS = 1e-08
WEIGHT_DECAY = 0.1


def entering(array, axis, combine, identity):
    peers, place = (lax.axis_size(axis), lax.axis_index(axis))
    everything = jax.tree.map(lambda part: lax.all_gather(part, axis), array)
    start = jax.tree.map(
        lambda part, zero: jnp.broadcast_to(jnp.asarray(zero, part.dtype), part.shape),
        array,
        identity,
    )

    def hop(k, before):
        reached = k < place
        new = combine(before, jax.tree.map(lambda part: part[k], everything))
        return jax.tree.map(lambda a, b: jnp.where(reached, a, b), new, before)

    return lax.fori_loop(0, peers, hop, start)


def entering_2(array, axis, join, neutral):
    count = lax.axis_size(axis)
    place = lax.axis_index(axis)
    ahead = count - 1 - place
    gathered = jax.tree.map(
        lambda a, kind: lax.all_gather(a.astype(kind), axis), array, (jnp.bfloat16, jnp.bfloat16)
    )
    state = jax.tree.map(lambda a, e: jnp.zeros_like(a) + jnp.asarray(e, a.dtype), array, neutral)

    def one(hop, state):
        source = count - 1 - hop
        return join(
            state,
            jax.tree.map(
                lambda a, own: lax.dynamic_index_in_dim(a, source, 0, False).astype(own.dtype),
                gathered,
                array,
            ),
        )

    return lax.fori_loop(0, ahead, one, state)


def decay_mask(cumul):
    along = jnp.swapaxes(cumul, 1, 2)
    spread = along[:, :, :, None] - along[:, :, None, :]
    length = cumul.shape[1]
    lower = jnp.tril(jnp.ones((length, length), jnp.float32))
    return jnp.exp(jnp.minimum(spread, 0.0)) * lower


def forward_join(earlier, later):
    return (earlier[0] * later[0], later[0][:, None, None] * earlier[1] + later[1])


def backward_join(earlier, later):
    return (earlier[0] * later[0], later[1] + later[0][:, None, None] * earlier[1])


def per_device(
    queries,
    keys,
    values,
    gate_pre,
    log_decay,
    out_grad,
    out_weight,
    moment_one,
    moment_two,
    group_ids,
    step_count,
):
    tok_local = queries.shape[1]
    head_local = log_decay.shape[2]
    width_local = queries.shape[2]
    blocks = tok_local // SPAN
    shaped = (blocks, SPAN, head_local, HEAD_DIM)
    query_c = queries.reshape(shaped)
    key_c = keys.reshape(shaped)
    value_c = values.reshape(shaped)
    cumul = jnp.cumsum(log_decay.reshape(blocks, SPAN, head_local), axis=1)
    totals = cumul[:, -1, :]
    masking = decay_mask(cumul)
    decay_in = jnp.exp(cumul)[..., None]
    decay_out = jnp.exp(totals[:, None, :] - cumul)[..., None]
    scores = jnp.einsum("cthe,cuhe->chtu", query_c, key_c, preferred_element_type=jnp.float32)
    probs = (scores * masking).astype(jnp.bfloat16)
    intra = jnp.einsum("chtu,cuhe->cthe", probs, value_c, preferred_element_type=jnp.float32)
    scaled = (decay_out * key_c).astype(jnp.bfloat16)
    updates = jnp.einsum("cthe,cthf->chef", scaled, value_c, preferred_element_type=jnp.float32)
    running = jnp.zeros((head_local, HEAD_DIM, HEAD_DIM), jnp.float32)
    leading = jnp.zeros((head_local,), jnp.float32)
    start_list = []
    lead_list = []
    for block in range(blocks):
        start_list.append(running)
        lead_list.append(leading)
        running = jnp.exp(totals[block])[:, None, None] * running + updates[block]
        leading = leading + totals[block]
    local_start = jnp.stack(start_list)
    lead_sums = jnp.stack(lead_list)
    empty_state = jnp.zeros((head_local, HEAD_DIM, HEAD_DIM), jnp.float32)
    ones_gain = jnp.ones((head_local,), jnp.float32)
    _, incoming = entering(
        (jnp.exp(leading), running), "ctx", forward_join, (ones_gain, empty_state)
    )
    states = local_start + jnp.exp(lead_sums)[:, :, None, None] * incoming[None]
    rounded = states.astype(jnp.bfloat16)
    inter = decay_in * jnp.einsum(
        "cthe,chef->cthf", query_c, rounded, preferred_element_type=jnp.float32
    )
    attn = intra + inter
    square = jnp.mean(attn * attn, axis=-1, keepdims=True)
    inverse = lax.rsqrt(square + NORM_EPS)
    normed = attn * inverse
    silu_gate = jax.nn.silu(gate_pre.reshape(shaped).astype(jnp.float32))
    mixed = (normed * silu_gate).astype(jnp.bfloat16).reshape(tok_local, width_local)
    features = lax.all_gather(out_grad, "head", axis=2, tiled=True)[0]
    weight_b = out_weight.astype(jnp.bfloat16)
    columns = features
    mixed_grad = jnp.dot(
        columns,
        lax.all_gather(weight_b, ("ctx", "fsdp"), axis=0, tiled=True),
        preferred_element_type=jnp.float32,
    )
    columns = features
    grad_rows = lax.psum_scatter(
        jnp.einsum("td,th->dh", columns, mixed, preferred_element_type=jnp.float32),
        ("ctx", "fsdp"),
        scatter_dimension=0,
        tiled=True,
    )
    normed_grad = mixed_grad.reshape(shaped) * silu_gate
    inner = jnp.mean(normed_grad * normed, axis=-1, keepdims=True)
    attn_grad = (inverse * (normed_grad - normed * inner)).astype(jnp.bfloat16)
    inners = jnp.einsum("cthf,cuhf->chtu", attn_grad, value_c, preferred_element_type=jnp.float32)
    dprobs = (inners * masking).astype(jnp.bfloat16)
    qgrad = jnp.einsum("chtu,cuhe->cthe", dprobs, key_c, preferred_element_type=jnp.float32)
    kgrad = jnp.einsum("chtu,cthe->cuhe", dprobs, query_c, preferred_element_type=jnp.float32)
    vgrad = jnp.einsum("chtu,cthf->cuhf", probs, attn_grad, preferred_element_type=jnp.float32)
    weighted = (decay_in * query_c).astype(jnp.bfloat16)
    back_updates = jnp.einsum(
        "cthe,cthf->chef", weighted, attn_grad, preferred_element_type=jnp.float32
    )
    backing = jnp.zeros((head_local, HEAD_DIM, HEAD_DIM), jnp.float32)
    trailing = jnp.zeros((head_local,), jnp.float32)
    after_list = [None] * blocks
    trail_list = [None] * blocks
    for block in reversed(range(blocks)):
        after_list[block] = backing
        trail_list[block] = trailing
        backing = jnp.exp(totals[block])[:, None, None] * backing + back_updates[block]
        trailing = trailing + totals[block]
    local_after = jnp.stack(after_list)
    trail_sums = jnp.stack(trail_list)
    _, arriving = entering_2(
        (jnp.exp(leading), backing), "ctx", backward_join, (ones_gain, empty_state)
    )
    after_full = local_after + jnp.exp(trail_sums)[:, :, None, None] * arriving[None]
    back_b = after_full.astype(jnp.bfloat16)
    qgrad = qgrad + decay_in * jnp.einsum(
        "cthf,chef->cthe", attn_grad, rounded, preferred_element_type=jnp.float32
    )
    kgrad = kgrad + decay_out * jnp.einsum(
        "cuhf,chef->cuhe", value_c, back_b, preferred_element_type=jnp.float32
    )
    vgrad = vgrad + decay_out * jnp.einsum(
        "cuhe,chef->cuhf", key_c, back_b, preferred_element_type=jnp.float32
    )
    query_grad = qgrad.astype(jnp.bfloat16).reshape(1, tok_local, width_local)
    key_grad = kgrad.astype(jnp.bfloat16).reshape(1, tok_local, width_local)
    value_grad = vgrad.astype(jnp.bfloat16).reshape(1, tok_local, width_local)
    token_count = tok_local * lax.axis_size("ctx") * lax.axis_size("fsdp")
    grad = grad_rows / jnp.sqrt(jnp.float32(token_count))
    row_group = jnp.repeat(group_ids, ROW_BLOCK)[:, None]
    stepped = step_count[0].astype(jnp.float32)
    first = BETA_ONE * moment_one + (1.0 - BETA_ONE) * grad
    second = BETA_TWO * moment_two + (1.0 - BETA_TWO) * grad * grad
    correct_one = 1.0 - jnp.power(BETA_ONE, stepped)
    correct_two = 1.0 - jnp.power(BETA_TWO, stepped)
    active = row_group >= 1
    decayed = (row_group == 2).astype(jnp.float32)
    direction = (
        first / correct_one / (jnp.sqrt(second / correct_two) + ADAM_EPS)
        + WEIGHT_DECAY * decayed * out_weight
    )
    new_moment_one = jnp.where(active, first, moment_one)
    new_moment_two = jnp.where(active, second, moment_two)
    weight_step = jnp.where(active, direction, 0.0)
    return (query_grad, key_grad, value_grad, new_moment_one, new_moment_two, weight_step)


def solution(mesh):
    in_specs = (
        P("fsdp", "ctx", "head"),
        P("fsdp", "ctx", "head"),
        P("fsdp", "ctx", "head"),
        P("fsdp", "ctx", "head"),
        P("fsdp", "ctx", "head"),
        P("fsdp", "ctx", "head"),
        P(("ctx", "fsdp"), "head"),
        P(("ctx", "fsdp"), "head"),
        P(("ctx", "fsdp"), "head"),
        P(("ctx", "fsdp")),
        P(),
    )
    out_specs = (
        P("fsdp", "ctx", "head"),
        P("fsdp", "ctx", "head"),
        P("fsdp", "ctx", "head"),
        P(("ctx", "fsdp"), "head"),
        P(("ctx", "fsdp"), "head"),
        P(("ctx", "fsdp"), "head"),
    )
    return jax.shard_map(
        per_device, mesh=mesh, in_specs=in_specs, out_specs=out_specs, check_vma=False
    )
```

profile of v0, /device:TPU:4, one launch (start us, length us, event | category | flops | bytes accessed | tf_op | source)
XLA Modules:
  0.0 863.6 jit_solution(1575633204360036188)
XLA Ops:
  8.0 2.4 reduce-window.6
  11.7 1.2 reshape.193
  12.9 1.2 reshape.197
  20.6 2.3 reshape.204
  23.0 2.6 copy.210
  25.6 36.0 %all-gather = f32[16,1,4]{2,1,0:T(1,128)S(1)} all-gather(f32[1,1,4]{2,1,0:T(1,128)S(1)} %get-tuple-element.320), channel_id=1, replica_groups=mesh['ctx'=16,'fsdp'=4,'head'=4] {'ctx'}, dimensions={0}, use_global_device_ids=true | all-gather | bytes 272 | tf_op jit(solution)/shard_map/all_gather | solution.py:18
  61.6 33.4 %all-gather.7.cloned.1.call-done = f32[16,4,128,128]{3,2,1,0:T(8,128)} async-done(((f32[1,4,128,128]{3,2,1,0:T(8,128)}), f32[16,4,128,128]{3,2,1,0:T(8,128)}) %all-gather.7.cloned.1.call-update) | async-done | bytes 4194320 | tf_op jit(solution)/shard_map/all_gather | solution.py:18
  95.0 17.5 %while.29 = (s32[]{:T(128)}, f32[4,128,128]{2,1,0:T(8,128)S(1)}, s32[]{:T(128)}, f32[16,4]{1,0:T(8,128)S(1)}, f32[16,4,128,128]{3,2,1,0:T(8,128)}, /*index=5*/s32[]{:T(128)}, s32[]{:T(128)}) while((s32[]{:T(128)}, f32[4,128,128]{2,1,0:T(8,128)S(1)}, s32[]{:T(128)}, f32[16,4]{1,0:T(8,128)S(1)}, f32[16,4,128,128]{3,2,1,0:T(8,128)}, ...), condition=%wide.region_3.4_spmd.clone, body=%wide.region_2.3_spmd.clone.sunk | while | flops 262148 | bytes 786593 | solution.py:30
  97.2 1.1 fusion.50
  98.3 1.1 fusion.50
  100.5 1.1 fusion.50
  102.7 1.1 fusion.50
  104.9 1.1 fusion.50
  112.6 1.4 multiply_reduce_fusion.1
  114.0 283.4 %all-gather.11.cloned.1.call-done = bf16[4096,512]{1,0:T(8,128)(2,1)} async-done(((bf16[64,512]{1,0:T(8,128)(2,1)}), bf16[4096,512]{1,0:T(8,128)(2,1)}) %all-gather.11.cloned.1.call-update) | async-done | bytes 4194320 | tf_op jit(solution)/shard_map/all_gather | solution.py:135
  397.5 6.5 copy.208
  403.9 31.7 %all-gather.9.cloned.1.call-done = bf16[1,512,4096]{2,1,0:T(8,128)(2,1)} async-done(((bf16[1,512,1024]{2,1,0:T(8,128)(2,1)}), bf16[1,512,4096]{2,1,0:T(8,128)(2,1)}) %all-gather.9.cloned.1.call-update) | async-done | bytes 4194320 | tf_op jit(solution)/shard_map/all_gather | solution.py:130
  435.6 6.3 multiply_reduce_fusion
  442.0 1.9 multiply_convert_fusion.2
  445.4 7.8 convolution_bitcast_fusion
  453.2 9.1 %copy.254 = f32[4096,512]{1,0:T(8,128)} copy(f32[4096,512]{0,1:T(8,128)} %convolution_bitcast_fusion) | data formatting | bytes 16777216
  463.2 34.7 %all-gather.1 = bf16[16,1,4]{2,1,0:T(2,128)(2,1)S(1)} all-gather(bf16[1,1,4]{2,1,0:T(2,128)(2,1)S(1)} %copy-done.25), channel_id=1, replica_groups=mesh['ctx'=16,'fsdp'=4,'head'=4] {'ctx'}, dimensions={0}, use_global_device_ids=true | all-gather | bytes 136 | tf_op jit(solution)/shard_map/all_gather | solution.py:38
  500.9 1.7 multiply_convert_fusion
  503.5 1.1 fusion.10
  504.7 2.1 copy.216
  506.8 2.0 reshape.198
  508.8 1.6 convolution_bitcast_fusion.6
  510.4 1.7 convolution_bitcast_fusion.5
  512.1 6.4 all-gather.13.cloned.1.call-done
  518.5 15.9 %while.28 = (s32[]{:T(128)}, f32[4,128,128]{2,1,0:T(8,128)S(1)}, s32[]{:T(128)}, bf16[16,4,128,128]{3,2,1,0:T(8,128)(2,1)}, bf16[16,4]{1,0:T(8,128)(2,1)S(1)}, /*index=5*/s32[]{:T(128)}, s32[]{:T(128)}, s32[]{:T(128)}, s32[]{:T(128)}) while((s32[]{:T(128)}, f32[4,128,128]{2,1,0:T(8,128)S(1)}, s32[]{:T(128)}, ...), condition=%wide.region_7.8_spmd, body=%wide.region_6.7_spmd.sunk | while | flops 196618 | bytes 655555 | solution.py:53
  534.4 1.6 fusion.11
  539.2 314.2 %reduce-scatter.4.cloned.1.call-done = f32[64,512]{1,0:T(8,128)} async-done(((f32[4096,512]{1,0:T(8,128)}), f32[64,512]{1,0:T(8,128)}) %reduce-scatter.4.cloned.1.call-update) | async-done | bytes 131088
  (182 shorter events, 48.0 us)
Async XLA Ops:
  7.2 87.9 %all-gather.7.cloned.1.call-start = ((), (), s32[]{:S(2)}) async-start(), calls=%async_computation.1 | async-start | bytes 4456448 | tf_op jit(solution)/shard_map/all_gather | solution.py:18
  10.8 7.3 copy-start.15
  11.7 4.3 copy-start.19
  11.7 4.3 copy-start.21
  12.9 3.2 copy-start.10
  14.2 3.5 copy-start.11
  16.1 96.5 %copy-start.3 = (f32[1,4,128,128]{3,2,1,0:T(8,128)}, f32[1,4,128,128]{3,2,1,0:T(8,128)S(1)}, u32[]{:S(2)}) copy-start(f32[1,4,128,128]{3,2,1,0:T(8,128)S(1)} %get-tuple-element.311) | copy-start | bytes 786436
  16.1 381.4 %all-gather.11.cloned.1.call-start = ((), (), s32[]{:S(2)}) async-start(), calls=%async_computation.3 | async-start | bytes 4259840 | tf_op jit(solution)/shard_map/all_gather | solution.py:135
  16.9 418.8 %all-gather.9.cloned.1.call-start = ((), (), s32[]{:S(2)}) async-start(), calls=%async_computation.2 | async-start | bytes 5242880 | tf_op jit(solution)/shard_map/all_gather | solution.py:130
  17.6 500.9 %all-gather.13.cloned.1.call-start = ((), (), s32[]{:S(2)}) async-start(), calls=%async_computation.4 | async-start | bytes 2228224 | tf_op jit(solution)/shard_map/all_gather | solution.py:38
  17.7 1.1 copy-start.12
  18.8 1.3 copy-start
  18.8 1.2 copy-start.20
  19.3 42.3 %copy-start.27 = (f32[4]{0:T(128)S(1)}, f32[4]{0:T(128)}, u32[]{:S(2)}) copy-start(f32[4]{0:T(128)} %get-tuple-element.286) | copy-start | bytes 52
  61.6 52.4 %copy-start.17 = (f32[2,4]{1,0:T(2,128)}, f32[2,4]{1,0:T(2,128)S(1)}, u32[]{:S(2)}) copy-start(f32[2,4]{1,0:T(2,128)S(1)} %pad_exponential_fusion.1) | copy-start | bytes 100
  114.0 321.6 %copy-start.16 = (f32[2,256,4]{1,2,0:T(4,128)}, f32[2,256,4]{1,2,0:T(4,128)S(1)}, u32[]{:S(2)}) copy-start(f32[2,256,4]{1,2,0:T(4,128)S(1)} %add_rsqrt_fusion) | copy-start | bytes 24580
  397.5 38.2 %copy-start.1 = (f32[2,256,4,128]{1,3,2,0:T(8,128)S(1)}, f32[2,256,4,128]{1,3,2,0:T(8,128)}, u32[]{:S(2)}) copy-start(f32[2,256,4,128]{1,3,2,0:T(8,128)} %copy.210) | copy-start | bytes 3145732
  435.6 6.3 copy-start.2
  442.0 2.3 copy-start.22
  442.0 2.3 copy-start.28
  443.9 1.2 copy-start.6
  445.1 408.4 %reduce-scatter.4.cloned.1.call-start = ((), (), s32[]{:S(2)}) async-start(), calls=%async_computation.5 | async-start | bytes 8519680
  462.3 35.8 %copy-start.13 = (f32[64,512]{1,0:T(8,128)S(1)}, f32[64,512]{1,0:T(8,128)}, u32[]{:S(2)}) copy-start(f32[64,512]{1,0:T(8,128)} %param.22) | copy-start | bytes 393220
  462.3 36.7 %copy-start.14 = (f32[64,512]{1,0:T(8,128)S(1)}, f32[64,512]{1,0:T(8,128)}, u32[]{:S(2)}) copy-start(f32[64,512]{1,0:T(8,128)} %param.23) | copy-start | bytes 393220
  462.3 37.5 %copy-start.29 = (s32[2]{0:T(128)S(1)}, s32[2]{0:T(128)}, u32[]{:S(2)}) copy-start(s32[2]{0:T(128)} %param.24) | copy-start | bytes 28
  462.3 38.6 %copy-start.24 = (f32[4]{0:T(128)S(1)}, f32[4]{0:T(128)}, u32[]{:S(2)}) copy-start(f32[4]{0:T(128)} %get-tuple-element.285) | copy-start | bytes 52
  502.6 1.0 copy-start.4
  502.6 0.9 copy-start.18
  512.1 22.3 %copy-start.5 = (f32[1,4,128,128]{3,2,1,0:T(8,128)S(1)}, f32[1,4,128,128]{3,2,1,0:T(8,128)}, u32[]{:S(2)}) copy-start(f32[1,4,128,128]{3,2,1,0:T(8,128)} %get-tuple-element.309) | copy-start | bytes 786436
  537.4 317.0 %copy-start.7 = (f32[64,512]{0,1:T(8,128)S(1)}, f32[64,512]{0,1:T(8,128)}, u32[]{:S(2)}) copy-start(f32[64,512]{0,1:T(8,128)} %copy.236) | copy-start | bytes 393220
  537.4 317.1 %copy-start.8 = (f32[64,512]{0,1:T(8,128)S(1)}, f32[64,512]{0,1:T(8,128)}, u32[]{:S(2)}) copy-start(f32[64,512]{0,1:T(8,128)} %copy.231) | copy-start | bytes 393220
  537.4 317.1 %copy-start.9 = (f32[64,512]{0,1:T(8,128)S(1)}, f32[64,512]{0,1:T(8,128)}, u32[]{:S(2)}) copy-start(f32[64,512]{0,1:T(8,128)} %copy.234) | copy-start | bytes 393220
  (3 other events, 2.2 us)
Sparse Core Ops, SparseCore 0:
  16.2 78.7 all-gather.6
  97.4 300.0 all-gather.10
  399.3 36.2 all-gather.8
  445.2 73.1 all-gather.12
  520.8 332.5 reduce-scatter.3
where the time goes:
time: 865 us; the launch traced here: 864 us
  waiting for transfers between devices  670 us (77%)
  blocking collectives  70.8 us (8%)
  other arithmetic  40.5 us (5%)
  local copies, waits for them, and re-layouts  39.7 us (5%)
  matrix products  26.6 us (3%)
  between operations  15 us (2%)
    unnamed x6, waiting for transfers between devices  315 us
    all_gather x1, waiting for transfers between devices, per_device(): lax.all_gather(weight_b, ('ctx', 'fsdp'), axis=0, tiled=True)  283 us
    all_gather x1, blocking collectives, entering(): everything = jax.tree.map(lambda part: lax.all_gather(part, axis), array)  36 us
    all_gather x1, blocking collectives, entering_2(): lax.all_gather(a.astype(kind), axis)  34.7 us
    all_gather x1, waiting for transfers between devices, entering(): everything = jax.tree.map(lambda part: lax.all_gather(part, axis), array)  33.4 us
    all_gather x1, waiting for transfers between devices, per_device(): features = lax.all_gather(out_grad, 'head', axis=2, tiled=True)[0]  31.7 us
  transfers between devices with their start and end apart: 5, of which 5 were waited for; matrix products, arithmetic and copies ran while one was open for 10% of the time, Pallas kernels for 0%

commit v1 on v0

--- a/solution.py
+++ b/solution.py
@@ -11,6 +11,13 @@
 BETA_TWO = 0.95
 ADAM_EPS = 1e-08
 WEIGHT_DECAY = 0.1
+
+
+def swapped_in(x, axis, dim):
+    size = lax.axis_size(axis)
+    tiles = jnp.stack([x for _ in range(size)])
+    tiles = lax.all_to_all(tiles, axis, split_axis=0, concat_axis=0)
+    return jnp.concatenate(tiles, axis=dim)
 
 
 def entering(array, axis, combine, identity):
@@ -131,9 +138,7 @@
     weight_b = out_weight.astype(jnp.bfloat16)
     columns = features
     mixed_grad = jnp.dot(
-        columns,
-        lax.all_gather(weight_b, ("ctx", "fsdp"), axis=0, tiled=True),
-        preferred_element_type=jnp.float32,
+        columns, swapped_in(weight_b, ("ctx", "fsdp"), 0), preferred_element_type=jnp.float32
     )
     columns = features
     grad_rows = lax.psum_scatter(

time: 865 us -> 637 us (0.74)
  waiting for transfers between devices: 670 us -> 321 us
  blocking collectives: 70.8 us -> 178 us
  starting transfers between devices: 0.2 us -> 13.3 us
    all_gather x1 -> x0, waiting for transfers between devices: 283 us -> none  [per_device(): lax.all_gather(weight_b, ('ctx', 'fsdp'), axis=0, tiled=True)]
    all_gather x1, blocking collectives: 36 us -> 148 us  [entering(): everything = jax.tree.map(lambda part: lax.all_gather(part, axis), array)]
    all_gather x1, waiting for transfers between devices: 33.4 us -> 0.02 us  [entering(): everything = jax.tree.map(lambda part: lax.all_gather(part, axis), array)]
    all_gather x1, waiting for transfers between devices: 31.7 us -> 0.01 us  [per_device(): features = lax.all_gather(out_grad, 'head', axis=2, tiled=True)[0]]
    all_to_all x0 -> x1, starting transfers between devices: none -> 13.1 us  [swapped_in(): tiles = lax.all_to_all(tiles, axis, split_axis=0, concat_axis=0)]
    unnamed x6 -> x5, waiting for transfers between devices: 315 us -> 315 us
  transfers between devices with their start and end apart: 5 -> 5, of which waited for: 5 -> 2; matrix products, arithmetic and copies ran while one was open for 10% -> 13% of each run, Pallas kernels for 0% -> 0%
where the time goes in v1:
time: 637 us; the launch traced here: 635 us
  waiting for transfers between devices  321 us (50%)
  blocking collectives  178 us (28%)
  local copies, waits for them, and re-layouts  41.9 us (7%)
  other arithmetic  40 us (6%)
  matrix products  25.3 us (4%)
  between operations  15 us (2%)
  starting transfers between devices  13.3 us (2%)
    unnamed x5, waiting for transfers between devices  315 us
    all_gather x1, blocking collectives, entering(): everything = jax.tree.map(lambda part: lax.all_gather(part, axis), array)  148 us
    all_gather x1, blocking collectives, entering_2(): lax.all_gather(a.astype(kind), axis)  29.7 us
    select_n x16, other arithmetic, hop(): return jax.tree.map(lambda a, b: jnp.where(reached, a, b), new, before)  16.9 us
    unnamed x72, local copies, waits for them, and re-layouts  16 us
    add x15, other arithmetic, backward_join(): later[1] + later[0][:, None, None] * earlier[1]  15.3 us
    all_to_all x1, starting transfers between devices, swapped_in(): tiles = lax.all_to_all(tiles, axis, split_axis=0, concat_axis=0)  13.1 us
  transfers between devices with their start and end apart: 5, of which 2 were waited for; matrix products, arithmetic and copies ran while one was open for 13% of the time, Pallas kernels for 0%

profile of v1, /device:TPU:4, one launch (start us, length us, event | category | flops | bytes accessed | tf_op | source)
XLA Modules:
  0.0 634.8 jit_solution(7822206711690761333)
XLA Ops:
  8.0 2.4 reduce-window.6
  11.3 1.2 reshape.198
  12.4 1.2 reshape.202
  15.6 2.5 stack.12
  18.1 13.1 %all-to-all-start = ((bf16[64,64,512]{2,1,0:T(8,128)(2,1)}), bf16[64,64,512]{2,1,0:T(8,128)(2,1)}, u32[]{:S(2)}, u32[]{:S(2)}) async-start(bf16[64,64,512]{2,1,0:T(8,128)(2,1)} %stack.12), calls=%async_computation | async-start | bytes 8388608 | tf_op jit(solution)/shard_map/all_to_all | solution.py:19
  35.4 2.3 reshape.210
  37.7 2.6 copy.210
  40.3 147.9 %all-gather = f32[16,1,4]{2,1,0:T(1,128)S(1)} all-gather(f32[1,1,4]{2,1,0:T(1,128)S(1)} %copy-done.29), channel_id=1, replica_groups=mesh['ctx'=16,'fsdp'=4,'head'=4] {'ctx'}, dimensions={0}, use_global_device_ids=true | all-gather | bytes 272 | tf_op jit(solution)/shard_map/all_gather | solution.py:25
  188.2 17.6 %while.29 = (s32[]{:T(128)}, f32[4,128,128]{2,1,0:T(8,128)S(1)}, s32[]{:T(128)}, f32[16,4]{1,0:T(8,128)S(1)}, f32[16,4,128,128]{3,2,1,0:T(8,128)}, /*index=5*/s32[]{:T(128)}, s32[]{:T(128)}) while((s32[]{:T(128)}, f32[4,128,128]{2,1,0:T(8,128)S(1)}, s32[]{:T(128)}, f32[16,4]{1,0:T(8,128)S(1)}, f32[16,4,128,128]{3,2,1,0:T(8,128)}, ...), condition=%wide.region_3.4_spmd.clone, body=%wide.region_2.3_spmd.clone.sunk | while | flops 262148 | bytes 786593 | solution.py:37
  188.3 1.1 fusion.50
  189.4 1.1 fusion.50
  191.5 1.1 fusion.50
  192.6 1.1 fusion.50
  194.9 1.1 fusion.50
  197.1 1.1 fusion.50
  198.2 1.1 fusion.50
  205.8 1.4 multiply_reduce_fusion.1
  207.3 6.4 %copy.208 = bf16[512,4096]{1,0:T(8,128)(2,1)} copy(bf16[512,4096]{0,1:T(8,128)(2,1)} %bitcast.13) | data formatting | bytes 8388608 | tf_op jit(solution)/shard_map/dot_general | solution.py:140
  213.7 6.3 multiply_reduce_fusion
  220.1 1.9 multiply_convert_fusion.2
  223.6 7.8 %convolution_bitcast_fusion = f32[4096,512]{0,1:T(8,128)} fusion(bf16[1,512,4096]{2,1,0:T(8,128)(2,1)} %all-gather.8.cloned.1.call-done, bf16[64,8,4,128]{3,2,1,0:T(4,128)(2,1)S(1)} %bitcast.124), kind=kOutput, calls=%fused_computation.5 | convolution fusion | flops 2147483648 | bytes 13107200 | tf_op jit(solution)/shard_map/td,th->dh/dot_general | solution.py:145
  231.3 9.1 %copy.254 = f32[4096,512]{1,0:T(8,128)} copy(f32[4096,512]{0,1:T(8,128)} %convolution_bitcast_fusion) | data formatting | bytes 16777216
  241.3 29.7 %all-gather.1 = bf16[16,1,4]{2,1,0:T(2,128)(2,1)S(1)} all-gather(bf16[1,1,4]{2,1,0:T(2,128)(2,1)S(1)} %copy-done.26), channel_id=1, replica_groups=mesh['ctx'=16,'fsdp'=4,'head'=4] {'ctx'}, dimensions={0}, use_global_device_ids=true | all-gather | bytes 136 | tf_op jit(solution)/shard_map/all_gather | solution.py:45
  274.0 1.7 multiply_convert_fusion
  276.6 1.1 fusion.10
  277.8 2.1 copy.216
  279.8 2.0 reshape.204
  281.9 1.6 convolution_bitcast_fusion.6
  284.0 5.8 all-gather.10.cloned.1.call-done
  289.8 15.9 %while.28 = (s32[]{:T(128)}, f32[4,128,128]{2,1,0:T(8,128)S(1)}, s32[]{:T(128)}, bf16[16,4,128,128]{3,2,1,0:T(8,128)(2,1)}, bf16[16,4]{1,0:T(8,128)(2,1)S(1)}, /*index=5*/s32[]{:T(128)}, s32[]{:T(128)}, s32[]{:T(128)}, s32[]{:T(128)}) while((s32[]{:T(128)}, f32[4,128,128]{2,1,0:T(8,128)S(1)}, s32[]{:T(128)}, ...), condition=%wide.region_7.8_spmd, body=%wide.region_6.7_spmd.sunk | while | flops 196618 | bytes 655555 | solution.py:60
  305.8 1.6 fusion.11
  310.6 314.1 %reduce-scatter.4.cloned.1.call-done = f32[64,512]{1,0:T(8,128)} async-done(((f32[4096,512]{1,0:T(8,128)}), f32[64,512]{1,0:T(8,128)}) %reduce-scatter.4.cloned.1.call-update) | async-done | bytes 131088
  (186 shorter events, 45.5 us)
Async XLA Ops:
  7.2 181.0 %all-gather.6.cloned.1.call-start = ((), (), s32[]{:S(2)}) async-start(), calls=%async_computation.2 | async-start | bytes 4456448 | tf_op jit(solution)/shard_map/all_gather | solution.py:25
  10.8 22.3 %copy-start.16 = (f32[2,4,256]{2,1,0:T(4,128)}, f32[2,4,256]{2,1,0:T(4,128)S(1)}, u32[]{:S(2)}) copy-start(f32[2,4,256]{2,1,0:T(4,128)S(1)} %reduce_window_sum.24) | copy-start | bytes 24580
  11.2 4.4 copy-start.20
  11.2 4.4 copy-start.22
  11.2 21.3 %copy-start.24 = (f32[4]{0:T(128)}, f32[4]{0:T(128)S(1)}, u32[]{:S(2)}) copy-start(f32[4]{0:T(128)S(1)} %get-tuple-element.285) | copy-start | bytes 52
  11.3 21.3 %copy-start.27 = (f32[4]{0:T(128)}, f32[4]{0:T(128)S(1)}, u32[]{:S(2)}) copy-start(f32[4]{0:T(128)S(1)} %get-tuple-element.286) | copy-start | bytes 52
  12.4 3.2 copy-start.11
  15.6 190.2 %copy-start.4 = (f32[1,4,128,128]{3,2,1,0:T(8,128)}, f32[1,4,128,128]{3,2,1,0:T(8,128)S(1)}, u32[]{:S(2)}) copy-start(f32[1,4,128,128]{3,2,1,0:T(8,128)S(1)} %get-tuple-element.311) | copy-start | bytes 786436
  18.1 13.9 %copy-start.12 = (bf16[1,512,512]{2,1,0:T(8,128)(2,1)S(1)}, bf16[1,512,512]{2,1,0:T(8,128)(2,1)}, u32[]{:S(2)}) copy-start(bf16[1,512,512]{2,1,0:T(8,128)(2,1)} %param.15) | copy-start | bytes 1572868
  18.1 189.1 %all-to-all-start = ((bf16[64,64,512]{2,1,0:T(8,128)(2,1)}), bf16[64,64,512]{2,1,0:T(8,128)(2,1)}, u32[]{:S(2)}, u32[]{:S(2)}) async-start(bf16[64,64,512]{2,1,0:T(8,128)(2,1)} %stack.12), calls=%async_computation | async-start | bytes 8388608 | tf_op jit(solution)/shard_map/all_to_all | solution.py:19
  31.3 182.4 %all-gather.8.cloned.1.call-start = ((), (), s32[]{:S(2)}) async-start(), calls=%async_computation.3 | async-start | bytes 5242880 | tf_op jit(solution)/shard_map/all_gather | solution.py:137
  32.0 257.8 %all-gather.10.cloned.1.call-start = ((), (), s32[]{:S(2)}) async-start(), calls=%async_computation.4 | async-start | bytes 2228224 | tf_op jit(solution)/shard_map/all_gather | solution.py:45
  32.5 1.8 copy-start.13
  35.4 4.9 copy-start.29
  35.4 152.8 %copy-start.28 = (f32[4]{0:T(128)S(1)}, f32[4]{0:T(128)}, u32[]{:S(2)}) copy-start(f32[4]{0:T(128)} %copy-done.27) | copy-start | bytes 52
  188.2 19.1 %copy-start.18 = (f32[2,4]{1,0:T(2,128)}, f32[2,4]{1,0:T(2,128)S(1)}, u32[]{:S(2)}) copy-start(f32[2,4]{1,0:T(2,128)S(1)} %pad_exponential_fusion.1) | copy-start | bytes 100
  207.3 6.5 %copy-start.17 = (f32[2,256,4]{1,2,0:T(4,128)}, f32[2,256,4]{1,2,0:T(4,128)S(1)}, u32[]{:S(2)}) copy-start(f32[2,256,4]{1,2,0:T(4,128)S(1)} %add_rsqrt_fusion) | copy-start | bytes 24580
  207.3 6.4 %copy-start.2 = (f32[2,256,4,128]{1,3,2,0:T(8,128)S(1)}, f32[2,256,4,128]{1,3,2,0:T(8,128)}, u32[]{:S(2)}) copy-start(f32[2,256,4,128]{1,3,2,0:T(8,128)} %copy.210) | copy-start | bytes 3145732
  213.7 6.3 copy-start.3
  220.1 2.3 copy-start.23
  220.1 2.3 copy-start.30
  222.0 1.2 copy-start.7
  223.2 401.5 %reduce-scatter.4.cloned.1.call-start = ((), (), s32[]{:S(2)}) async-start(), calls=%async_computation.5 | async-start | bytes 8519680
  240.4 30.8 %copy-start.14 = (f32[64,512]{1,0:T(8,128)S(1)}, f32[64,512]{1,0:T(8,128)}, u32[]{:S(2)}) copy-start(f32[64,512]{1,0:T(8,128)} %param.22) | copy-start | bytes 393220
  240.4 31.6 %copy-start.15 = (f32[64,512]{1,0:T(8,128)S(1)}, f32[64,512]{1,0:T(8,128)}, u32[]{:S(2)}) copy-start(f32[64,512]{1,0:T(8,128)} %param.23) | copy-start | bytes 393220
  240.4 32.5 %copy-start.31 = (s32[2]{0:T(128)S(1)}, s32[2]{0:T(128)}, u32[]{:S(2)}) copy-start(s32[2]{0:T(128)} %param.24) | copy-start | bytes 28
  240.4 33.5 %copy-start.25 = (f32[4]{0:T(128)S(1)}, f32[4]{0:T(128)}, u32[]{:S(2)}) copy-start(f32[4]{0:T(128)} %copy-done.24) | copy-start | bytes 52
  281.9 1.6 copy-start.1
  283.9 21.8 %copy-start.6 = (f32[1,4,128,128]{3,2,1,0:T(8,128)S(1)}, f32[1,4,128,128]{3,2,1,0:T(8,128)}, u32[]{:S(2)}) copy-start(f32[1,4,128,128]{3,2,1,0:T(8,128)} %get-tuple-element.309) | copy-start | bytes 786436
  308.8 316.9 %copy-start.8 = (f32[64,512]{0,1:T(8,128)S(1)}, f32[64,512]{0,1:T(8,128)}, u32[]{:S(2)}) copy-start(f32[64,512]{0,1:T(8,128)} %copy.236) | copy-start | bytes 393220
  308.8 316.9 %copy-start.9 = (f32[64,512]{0,1:T(8,128)S(1)}, f32[64,512]{0,1:T(8,128)}, u32[]{:S(2)}) copy-start(f32[64,512]{0,1:T(8,128)} %copy.231) | copy-start | bytes 393220
  308.8 317.0 %copy-start.10 = (f32[64,512]{0,1:T(8,128)S(1)}, f32[64,512]{0,1:T(8,128)}, u32[]{:S(2)}) copy-start(f32[64,512]{0,1:T(8,128)} %copy.234) | copy-start | bytes 393220
  (5 other events, 4.8 us)
Sparse Core Ops, SparseCore 0:
  15.7 151.8 all-gather.5
  169.4 37.5 all-gather.7
  223.3 66.4 all-gather.9
  292.2 332.4 reduce-scatter.3
